TPU v7x, 32 devices: a whole 2x2x4 slice. The times are simulated.
32 devices in a mesh: sub: 8 (over z, x), coarse: 4 (over y, core).
Axes of the slice: x: 2, y: 2, z: 4, core: 2. Of those that a mesh axis runs over, the one named last changes fastest.
Arguments:
- residual: bfloat16 [128, 512, 256], P(('sub', 'coarse')), may hold values from -6 to 6
- margin: int32 [128, 4], P(('sub', 'coarse')), may hold values from 0 to 5, as said below
- inverse_blocks: bfloat16 [128, 4, 256, 256], P(('sub', 'coarse')), may hold values from -0.1875 to 0.1875
- interface: int32 [128, 2], P(('sub', 'coarse')), may hold values from 0 to 11, as said below
- basis: bfloat16 [128, 2, 256, 128], P(('sub', 'coarse')), may hold values from -0.375 to 0.375
- coarse_pattern: int32 [12, 4], P('coarse'), may hold values from 0 to 11, as said below
- coarse_inverse: bfloat16 [12, 4, 128, 128], P('coarse'), may hold values from -0.0546875 to 0.0546875
Outputs:
- correction: bfloat16 [128, 512, 256], P(('sub', 'coarse'))
Inputs may be any that keep to these rules, and one draw needn't show every extreme that they name: margin[j, 0] is j's own slot j % 4 + 1; the first block of each subdomain has slot 0 in entry 1 and the last has slot 5 in entry 2. interface[j, 0] = j % 12. coarse_pattern[n, 0] = n.
All inputs are finite; a program needn't handle non-finite values.
Results may differ from a plain program's by a relative error of at most 0.0051.
Values may be sent and summed in bfloat16 or wider, within the bound.
No kernel may reach another device: no remote copies, remote signals or barrier semaphores. Data moves between devices by JAX's collectives and lax.ppermute only.
A program may use at most 64 MiB of HBM per device.

v0:
```python
import jax
import jax.numpy as jnp
from jax import lax
from jax.sharding import PartitionSpec as P


def with_halo(cells, sides, width):
    for axis, dim in sides:
        count = lax.axis_size(axis)
        ends = count - 1
        head = lax.slice_in_dim(cells, 0, width, axis=dim)
        tail = lax.slice_in_dim(cells, cells.shape[dim] - width, cells.shape[dim], axis=dim)
        cells = jnp.concatenate(
            [
                lax.ppermute(tail, axis, [(i, (i + 1) % count) for i in range(ends)]),
                cells,
                lax.ppermute(head, axis, [((i + 1) % count, i) for i in range(ends)]),
            ],
            axis=dim,
        )
    return cells


def coarse_rows(inputs, coarse_pattern, coarse_inverse):
    chosen = jnp.take(inputs, coarse_pattern, axis=0)
    return jnp.einsum(
        "nerc,necd->nrd", chosen, coarse_inverse, preferred_element_type=jnp.float32
    ).astype(jnp.bfloat16)


def per_device(residual, margin, inverse_blocks, interface, basis, coarse_pattern, coarse_inverse):
    extended = with_halo(residual, ((("sub", "coarse"), 0),), 1)
    terms = jnp.einsum("jrb,jqbc->jqrc", residual, basis, preferred_element_type=jnp.float32)
    total_blocks = coarse_pattern.shape[0] * lax.axis_size("coarse")
    labels = jnp.arange(total_blocks, dtype=jnp.int32)
    onehot = (interface[:, :, None] == labels[None, None, :]).astype(jnp.float32)
    restricted = jnp.einsum("jqn,jqrc->nrc", onehot, terms, precision=lax.Precision.HIGHEST)
    picked = jnp.take(extended, margin, axis=0)
    local = jnp.einsum("jerb,jebc->jrc", picked, inverse_blocks, preferred_element_type=jnp.float32)
    shares = lax.psum_scatter(restricted, "coarse", scatter_dimension=0, tiled=True)
    shares = lax.psum(shares, "sub")
    inputs = lax.all_gather(shares.astype(jnp.bfloat16), "coarse", axis=0, tiled=True)
    owned = coarse_rows(inputs, coarse_pattern, coarse_inverse)
    coarse_out = lax.all_gather(owned, "coarse", axis=0, tiled=True)
    lifted = jnp.take(coarse_out, interface, axis=0)
    spread = jnp.einsum("jqrc,jqbc->jrb", lifted, basis, preferred_element_type=jnp.float32)
    return (local + spread).astype(jnp.bfloat16)


def solution(mesh):
    in_specs = (
        P(("sub", "coarse"), None, None),
        P(("sub", "coarse"), None),
        P(("sub", "coarse"), None, None, None),
        P(("sub", "coarse"), None),
        P(("sub", "coarse"), None, None, None),
        P("coarse", None),
        P("coarse", None, None, None),
    )
    out_specs = P(("sub", "coarse"), None, None)
    return jax.shard_map(
        per_device, mesh=mesh, in_specs=in_specs, out_specs=out_specs, check_vma=False
    )
```

profile of v0, /device:TPU:6, one launch (start us, length us, event | category | flops | bytes accessed | tf_op | source)
XLA Modules:
  0.0 169.5 jit_solution(14236015216186397533)
XLA Ops:
  6.5 3.4 %convolution_bitcast_fusion.1 = f32[4,2,512,128]{2,3,1,0:T(8,128)} fusion(bf16[4,2,256,128]{3,2,1,0:T(8,128)(2,1)} %param.11, bf16[4,512,256]{2,1,0:T(8,128)(2,1)} %param.7), kind=kOutput, calls=%fused_computation.10 | convolution fusion | flops 268435456 | bytes 3670016 | tf_op jit(solution)/shard_map/jrb,jqbc->jqrc/dot_general | solution.py:33
  9.9 2.9 %copy.16 = f32[4,2,512,128]{3,0,1,2:T(4,128)} copy(f32[4,2,512,128]{2,3,1,0:T(8,128)} %convolution_bitcast_fusion.1) | data formatting | bytes 4194304 | tf_op jit(solution)/shard_map/jrb,jqbc->jqrc/transpose | solution.py:33
  12.8 4.1 %convolution_bitcast_fusion = f32[12,512,128]{2,0,1:T(8,128)S(1)} fusion(f32[4,2,512,128]{3,0,1,2:T(4,128)} %copy.16, s32[4,2]{0,1:T(2,128)S(1)} %copy-done.4), kind=kOutput, calls=%fused_computation.6 | convolution fusion | flops 75497568 | bytes 5242912 | tf_op jit(solution)/shard_map/jqn,jqrc->nrc/dot_general | solution.py:37
  17.0 2.6 %copy.17 = f32[12,512,128]{2,1,0:T(8,128)} copy(f32[12,512,128]{2,0,1:T(8,128)S(1)} %convolution_bitcast_fusion) | data formatting | bytes 6291456 | tf_op jit(solution)/shard_map/jqn,jqrc->nrc/dot_general | solution.py:37
  19.6 38.3 %reduce-scatter.2.cloned.1.call-done = f32[3,512,128]{2,1,0:T(8,128)} async-done(((f32[12,512,128]{2,1,0:T(8,128)}), f32[3,512,128]{2,1,0:T(8,128)}) %reduce-scatter.2.cloned.1.call-update) | async-done | bytes 786448 | tf_op jit(solution)/shard_map/reduce_scatter | solution.py:40
  58.0 44.8 %all-reduce.1 = bf16[3,512,128]{2,1,0:T(8,128)(2,1)} all-reduce(f32[3,512,128]{2,1,0:T(8,128)} %reduce-scatter.2.cloned.1.call-done), channel_id=1, replica_groups=mesh['sub'=8,'coarse'=4] {'sub'}, use_global_device_ids=true, to_apply=%region_1.2 | all-reduce | flops 196608 | bytes 1179648 | tf_op jit(solution)/shard_map/psum | solution.py:41
  102.8 0.1 reshape.26
  102.9 19.7 %all-gather.3.cloned.1.call-done = bf16[12,512,128]{2,1,0:T(8,128)(2,1)} async-done(((bf16[3,512,128]{2,1,0:T(8,128)(2,1)}), bf16[12,512,128]{2,1,0:T(8,128)(2,1)}) %all-gather.3.cloned.1.call-update) | async-done | bytes 1572880 | tf_op jit(solution)/shard_map/all_gather | solution.py:42
  122.6 3.4 %gather_fusion.1 = bf16[12,512,128]{2,1,0:T(8,128)(2,1)} fusion(bf16[12,512,128]{2,1,0:T(8,128)(2,1)} %all-gather.3.cloned.1.call-done, s32[1024]{0:T(1024)S(1)} %pad_clamp_fusion.1), kind=kCustom, calls=%fused_computation.1 | custom fusion | bytes 3145776 | tf_op jit(solution)/shard_map/jit(_take)/gather | solution.py:25
  126.0 2.9 %fusion.13 = bf16[3,512,128]{2,1,0:T(8,128)(2,1)} fusion(bf16[3,4,128,128]{3,2,1,0:T(8,128)(2,1)} %param.13, bf16[3,4,512,128]{3,2,1,0:T(8,128)(2,1)} %bitcast.36, pred[3,4]{1,0:T(4,128)(4,1)S(1)} %compare_and_fusion), kind=kOutput, calls=%fused_computation.16 | convolution fusion | flops 202309632 | bytes 2359308 | tf_op jit(solution)/shard_map/nerc,necd->nrd/dot_general | solution.py:26
  128.9 0.8 fusion.28
  129.8 3.2 %collective-permute-start.1 = (bf16[1,512,256]{2,1,0:T(8,128)(2,1)}, bf16[1,512,256]{2,1,0:T(8,128)(2,1)S(1)}, u32[]{:S(2)}, u32[]{:S(2)}) collective-permute-start(bf16[1,512,256]{2,1,0:T(8,128)(2,1)} %get-tuple-element.6), channel_id=1, source_target_pairs={{1,0},{2,1},{3,2},{4,3},{5,4},{6,5},{7,6},{8,7},{9,8},{10,9},{11,1... | collective-permute-start | bytes 786440 | tf_op jit(solution)/shard_map/ppermute | solution.py:17
  133.0 1.9 %collective-permute-start = (bf16[1,512,256]{2,1,0:T(8,128)(2,1)}, bf16[1,512,256]{2,1,0:T(8,128)(2,1)}, u32[]{:S(2)}, u32[]{:S(2)}) collective-permute-start(bf16[1,512,256]{2,1,0:T(8,128)(2,1)} %get-tuple-element.5), channel_id=1, source_target_pairs={{0,1},{1,2},{2,3},{3,4},{4,5},{5,6},{6,7},{7,8},{8,9},{9,10},{10,1... | collective-permute-start | bytes 786440 | tf_op jit(solution)/shard_map/ppermute | solution.py:15
  134.9 0.1 copy.18
  135.0 0.1 reshape.34
  135.1 0.1 reshape.18
  135.2 0.1 copy.14
  135.4 1.9 %collective-permute-done.1 = bf16[1,512,256]{2,1,0:T(8,128)(2,1)S(1)} collective-permute-done((bf16[1,512,256]{2,1,0:T(8,128)(2,1)}, bf16[1,512,256]{2,1,0:T(8,128)(2,1)S(1)}, u32[]{:S(2)}, u32[]{:S(2)}) %collective-permute-start.1) | collective-permute-done | bytes 262176 | tf_op jit(solution)/shard_map/ppermute | solution.py:17
  137.2 11.0 %collective-permute-done = bf16[1,512,256]{2,1,0:T(8,128)(2,1)} collective-permute-done((bf16[1,512,256]{2,1,0:T(8,128)(2,1)}, bf16[1,512,256]{2,1,0:T(8,128)(2,1)}, u32[]{:S(2)}, u32[]{:S(2)}) %collective-permute-start) | collective-permute-done | bytes 262176 | tf_op jit(solution)/shard_map/ppermute | solution.py:15
  148.3 2.3 %pad_maximum_fusion = bf16[6,512,256]{2,1,0:T(8,128)(2,1)} fusion(bf16[1,512,256]{2,1,0:T(8,128)(2,1)S(1)} %collective-permute-done.1, bf16[4,512,256]{2,1,0:T(8,128)(2,1)S(1)} %copy-done.1, bf16[1,512,256]{2,1,0:T(8,128)(2,1)} %collective-permute-done), kind=kLoop, calls=%fused_computation.11 | loop fusion | flops 1572864 | bytes 3145728 | tf_op jit(solution)/shard_map/concatenate | solution.py:13
  150.6 4.2 %gather_fusion = bf16[16,512,256]{2,1,0:T(8,128)(2,1)} fusion(bf16[6,512,256]{2,1,0:T(8,128)(2,1)} %pad_maximum_fusion, s32[1024]{0:T(1024)S(1)} %pad_clamp_fusion.2), kind=kCustom, calls=%fused_computation | custom fusion | bytes 8388672 | tf_op jit(solution)/shard_map/jit(_take)/gather | solution.py:38
  154.8 2.2 %gather_fusion.2 = bf16[8,512,128]{2,1,0:T(8,128)(2,1)S(1)} fusion(bf16[12,512,128]{2,1,0:T(8,128)(2,1)} %all-gather.5.cloned.1.call-done, s32[1024]{0:T(1024)S(1)} %pad_clamp_fusion), kind=kCustom, calls=%fused_computation.2 | custom fusion | bytes 2097184 | tf_op jit(solution)/shard_map/jit(_take)/gather | solution.py:45
  156.9 1.5 fusion.17
  158.5 4.5 %fusion.3 = bf16[4,512,256]{2,1,0:T(8,128)(2,1)} fusion(f32[4,512,256,1]{2,1,3,0:T(8,128)S(1)} %fusion.17, bf16[4,4,256,256]{3,2,1,0:T(8,128)(2,1)S(1)} %copy-done, bf16[4,4,512,256]{3,2,1,0:T(8,128)(2,1)} %bitcast.34, pred[4,4]{1,0:T(4,128)(4,1)S(1)} %compare_and_fusion.2), kind=kOutput, calls=%fused_computation.8 | convolution fusion | flops 1076887552 | bytes 9437200 | tf_op jit(solution)/shard_map/jerb,jebc->jrc/dot_general | solution.py:39
  (26 shorter events, 0.2 us)
Async XLA Ops:
  6.5 151.9 %copy-start = (bf16[4,4,256,256]{3,2,1,0:T(8,128)(2,1)S(1)}, bf16[4,4,256,256]{3,2,1,0:T(8,128)(2,1)}, u32[]{:S(2)}) copy-start(bf16[4,4,256,256]{3,2,1,0:T(8,128)(2,1)} %param.9) | copy-start | bytes 6291460
  6.5 51.4 %reduce-scatter.2.cloned.1.call-start = ((), (), s32[]{:S(2)}) async-start(), calls=%async_computation.1 | async-start | bytes 3932160 | tf_op jit(solution)/shard_map/reduce_scatter | solution.py:40
  9.9 2.9 %copy-start.4 = (s32[4,2]{0,1:T(2,128)S(1)}, s32[4,2]{0,1:T(2,128)}, u32[]{:S(2)}) copy-start(s32[4,2]{0,1:T(2,128)} %param.10) | copy-start | bytes 100
  19.6 83.3 %copy-start.2 = (s32[3,4]{1,0:T(4,128)S(1)}, s32[3,4]{1,0:T(4,128)}, u32[]{:S(2)}) copy-start(s32[3,4]{1,0:T(4,128)} %param.12) | copy-start | bytes 148
  19.6 103.0 %all-gather.3.cloned.1.call-start = ((), (), s32[]{:S(2)}) async-start(), calls=%async_computation.2 | async-start | bytes 1966080 | tf_op jit(solution)/shard_map/all_gather | solution.py:42
  102.8 52.0 %all-gather.5.cloned.1.call-start = ((), (), s32[]{:S(2)}) async-start(), calls=%async_computation.3 | async-start | bytes 1966080 | tf_op jit(solution)/shard_map/all_gather | solution.py:44
  126.0 3.0 %copy-start.1 = (bf16[4,512,256]{2,1,0:T(8,128)(2,1)S(1)}, bf16[4,512,256]{2,1,0:T(8,128)(2,1)}, u32[]{:S(2)}) copy-start(bf16[4,512,256]{2,1,0:T(8,128)(2,1)} %param.7) | copy-start | bytes 3145732
  126.0 9.2 %copy-start.3 = (s32[4,4]{1,0:T(4,128)S(1)}, s32[4,4]{1,0:T(4,128)}, u32[]{:S(2)}) copy-start(s32[4,4]{1,0:T(4,128)} %param.8) | copy-start | bytes 196
  129.8 7.4 %collective-permute-start.1 = (bf16[1,512,256]{2,1,0:T(8,128)(2,1)}, bf16[1,512,256]{2,1,0:T(8,128)(2,1)S(1)}, u32[]{:S(2)}, u32[]{:S(2)}) collective-permute-start(bf16[1,512,256]{2,1,0:T(8,128)(2,1)} %get-tuple-element.6), channel_id=1, source_target_pairs={{1,0},{2,1},{3,2},{4,3},{5,4},{6,5},{7,6},{8,7},{9,8},{10,9},{11,1... | collective-permute-start | bytes 786440 | tf_op jit(solution)/shard_map/ppermute | solution.py:17
  133.0 15.3 %collective-permute-start = (bf16[1,512,256]{2,1,0:T(8,128)(2,1)}, bf16[1,512,256]{2,1,0:T(8,128)(2,1)}, u32[]{:S(2)}, u32[]{:S(2)}) collective-permute-start(bf16[1,512,256]{2,1,0:T(8,128)(2,1)} %get-tuple-element.5), channel_id=1, source_target_pairs={{0,1},{1,2},{2,3},{3,4},{4,5},{5,6},{6,7},{7,8},{8,9},{9,10},{10,1... | collective-permute-start | bytes 786440 | tf_op jit(solution)/shard_map/ppermute | solution.py:15
Sparse Core Ops, SparseCore 0:
  19.7 38.1 reduce-scatter.1
  102.9 19.6 all-gather.2
  129.0 23.5 all-gather.4
where the time goes:
time: 170 us; the launch traced here: 169 us
  waiting for transfers between devices  71 us (42%)
  blocking collectives  44.8 us (26%)
  local copies, waits for them, and re-layouts  16.5 us (10%)
  matrix products  16.4 us (10%)
  between operations  13.2 us (8%)
  starting transfers between devices  5.22 us (3%)
  other arithmetic  2.37 us (1%)
    psum x1, blocking collectives, per_device(): shares = lax.psum(shares, 'sub')  44.8 us
    reduce_scatter x1, waiting for transfers between devices, per_device(): lax.psum_scatter(restricted, 'coarse', scatter_dimension=0, tiled=True)  38.3 us
    all_gather x1, waiting for transfers between devices, per_device(): lax.all_gather(shares.astype(jnp.bfloat16), 'coarse', axis=0, tiled=True)  19.7 us
    ppermute x1, waiting for transfers between devices, with_halo(): lax.ppermute(tail, axis, [(i, (i + 1) % count) for i in range(ends)])  11 us
    dot_general x1, matrix products, per_device(): jnp.einsum('jerb,jebc->jrc', picked, inverse_blocks, preferred_element_ty...  4.48 us
    gather x1, local copies, waits for them, and re-layouts, per_device(): picked = jnp.take(extended, margin, axis=0)  4.18 us
    dot_general x1, matrix products, per_device(): jnp.einsum('jqn,jqrc->nrc', onehot, terms, precision=lax.Precision.HIGHEST)  4.12 us
  transfers between devices with their start and end apart: 5, of which 4 were waited for; matrix products, arithmetic and copies ran while one was open for 5% of the time, Pallas kernels for 0%

commit v1 on v0

--- a/solution.py
+++ b/solution.py
@@ -38,7 +38,8 @@
     picked = jnp.take(extended, margin, axis=0)
     local = jnp.einsum("jerb,jebc->jrc", picked, inverse_blocks, preferred_element_type=jnp.float32)
     shares = lax.psum_scatter(restricted, "coarse", scatter_dimension=0, tiled=True)
-    shares = lax.psum(shares, "sub")
+    pieces = lax.all_gather(shares, "sub")
+    shares = jnp.sum(pieces, axis=0)
     inputs = lax.all_gather(shares.astype(jnp.bfloat16), "coarse", axis=0, tiled=True)
     owned = coarse_rows(inputs, coarse_pattern, coarse_inverse)
     coarse_out = lax.all_gather(owned, "coarse", axis=0, tiled=True)

time: 170 us -> 229 us (1.35)
  waiting for transfers between devices: 71 us -> 171 us
  blocking collectives: 44.8 us -> 0 us
  other arithmetic: 2.37 us -> 6.33 us
    all_gather x0 -> x1, waiting for transfers between devices: none -> 101 us  [per_device(): pieces = lax.all_gather(shares, 'sub')]
    psum x1 -> x0, blocking collectives: 44.8 us -> none  [per_device(): shares = lax.psum(shares, 'sub')]
    reduce_sum x0 -> x1, other arithmetic: none -> 3.96 us  [per_device(): shares = jnp.sum(pieces, axis=0)]
  transfers between devices with their start and end apart: 5 -> 6, of which waited for: 4 -> 5; matrix products, arithmetic and copies ran while one was open for 5% -> 3% of each run, Pallas kernels for 0% -> 0%
where the time goes in v1:
time: 229 us; the launch traced here: 228 us
  waiting for transfers between devices  171 us (75%)
  local copies, waits for them, and re-layouts  16.5 us (7%)
  matrix products  16.4 us (7%)
  between operations  13.2 us (6%)
  other arithmetic  6.33 us (3%)
  starting transfers between devices  5.26 us (2%)
    all_gather x1, waiting for transfers between devices, per_device(): pieces = lax.all_gather(shares, 'sub')  101 us
    reduce_scatter x1, waiting for transfers between devices, per_device(): lax.psum_scatter(restricted, 'coarse', scatter_dimension=0, tiled=True)  38.3 us
    all_gather x1, waiting for transfers between devices, per_device(): lax.all_gather(shares.astype(jnp.bfloat16), 'coarse', axis=0, tiled=True)  17.8 us
    ppermute x1, waiting for transfers between devices, with_halo(): lax.ppermute(tail, axis, [(i, (i + 1) % count) for i in range(ends)])  11 us
  transfers between devices with their start and end apart: 6, of which 5 were waited for; matrix products, arithmetic and copies ran while one was open for 3% of the time, Pallas kernels for 0%

profile of v1, /device:TPU:6, one launch (start us, length us, event | category | flops | bytes accessed | tf_op | source)
XLA Modules:
  0.0 228.3 jit_solution(11721621654937100813)
XLA Ops:
  6.5 3.4 %convolution_bitcast_fusion.1 = f32[4,2,512,128]{2,3,1,0:T(8,128)} fusion(bf16[4,2,256,128]{3,2,1,0:T(8,128)(2,1)} %param.11, bf16[4,512,256]{2,1,0:T(8,128)(2,1)} %param.7), kind=kOutput, calls=%fused_computation.10 | convolution fusion | flops 268435456 | bytes 3670016 | tf_op jit(solution)/shard_map/jrb,jqbc->jqrc/dot_general | solution.py:33
  9.9 2.9 %copy.15 = f32[4,2,512,128]{3,0,1,2:T(4,128)} copy(f32[4,2,512,128]{2,3,1,0:T(8,128)} %convolution_bitcast_fusion.1) | data formatting | bytes 4194304 | tf_op jit(solution)/shard_map/jrb,jqbc->jqrc/transpose | solution.py:33
  12.8 4.1 %convolution_bitcast_fusion = f32[12,512,128]{2,0,1:T(8,128)S(1)} fusion(f32[4,2,512,128]{3,0,1,2:T(4,128)} %copy.15, s32[4,2]{0,1:T(2,128)S(1)} %copy-done.4), kind=kOutput, calls=%fused_computation.6 | convolution fusion | flops 75497568 | bytes 5242912 | tf_op jit(solution)/shard_map/jqn,jqrc->nrc/dot_general | solution.py:37
  17.0 2.6 %copy.16 = f32[12,512,128]{2,1,0:T(8,128)} copy(f32[12,512,128]{2,0,1:T(8,128)S(1)} %convolution_bitcast_fusion) | data formatting | bytes 6291456 | tf_op jit(solution)/shard_map/jqn,jqrc->nrc/dot_general | solution.py:37
  19.6 38.3 %reduce-scatter.2.cloned.1.call-done = f32[3,512,128]{2,1,0:T(8,128)} async-done(((f32[12,512,128]{2,1,0:T(8,128)}), f32[3,512,128]{2,1,0:T(8,128)}) %reduce-scatter.2.cloned.1.call-update) | async-done | bytes 786448 | tf_op jit(solution)/shard_map/reduce_scatter | solution.py:40
  58.0 101.4 %all-gather.9.cloned.1.call-done = f32[24,512,128]{2,1,0:T(8,128)} async-done(((f32[3,512,128]{2,1,0:T(8,128)}), f32[24,512,128]{2,1,0:T(8,128)}) %all-gather.9.cloned.1.call-update) | async-done | bytes 6291472 | tf_op jit(solution)/shard_map/all_gather | solution.py:41
  159.4 4.0 %reduce_sum.9 = bf16[3,512,128]{2,1,0:T(8,128)(2,1)} reduce(f32[8,3,512,128]{3,2,1,0:T(8,128)} %bitcast.35, f32[]{:T(128)} %constant.43.clone.1), dimensions={0}, to_apply=%region_1.2 | reduce | flops 1376256 | bytes 6684676 | tf_op jit(solution)/shard_map/reduce_sum | solution.py:42
  163.6 17.8 %all-gather.5.cloned.1.call-done = bf16[12,512,128]{2,1,0:T(8,128)(2,1)} async-done(((bf16[3,512,128]{2,1,0:T(8,128)(2,1)}), bf16[12,512,128]{2,1,0:T(8,128)(2,1)}) %all-gather.5.cloned.1.call-update) | async-done | bytes 1572880 | tf_op jit(solution)/shard_map/all_gather | solution.py:43
  181.4 3.3 %gather_fusion.1 = bf16[12,512,128]{2,1,0:T(8,128)(2,1)} fusion(bf16[12,512,128]{2,1,0:T(8,128)(2,1)} %all-gather.5.cloned.1.call-done, s32[1024]{0:T(1024)S(1)} %pad_clamp_fusion.1), kind=kCustom, calls=%fused_computation.1 | custom fusion | bytes 3145776 | tf_op jit(solution)/shard_map/jit(_take)/gather | solution.py:25
  184.8 2.9 %fusion.13 = bf16[3,512,128]{2,1,0:T(8,128)(2,1)} fusion(bf16[3,4,128,128]{3,2,1,0:T(8,128)(2,1)} %param.13, bf16[3,4,512,128]{3,2,1,0:T(8,128)(2,1)} %bitcast.38, pred[3,4]{1,0:T(4,128)(4,1)S(1)} %compare_and_fusion), kind=kOutput, calls=%fused_computation.16 | convolution fusion | flops 202309632 | bytes 2359308 | tf_op jit(solution)/shard_map/nerc,necd->nrd/dot_general | solution.py:26
  187.7 0.9 fusion.28
  188.6 3.2 %collective-permute-start.1 = (bf16[1,512,256]{2,1,0:T(8,128)(2,1)}, bf16[1,512,256]{2,1,0:T(8,128)(2,1)S(1)}, u32[]{:S(2)}, u32[]{:S(2)}) collective-permute-start(bf16[1,512,256]{2,1,0:T(8,128)(2,1)} %get-tuple-element.6), channel_id=1, source_target_pairs={{1,0},{2,1},{3,2},{4,3},{5,4},{6,5},{7,6},{8,7},{9,8},{10,9},{11,1... | collective-permute-start | bytes 786440 | tf_op jit(solution)/shard_map/ppermute | solution.py:17
  191.8 1.9 collective-permute-start
  193.7 0.1 copy.17
  193.8 0.1 reshape.34
  193.9 0.1 reshape.18
  194.0 0.1 copy.13
  194.2 1.9 collective-permute-done.1
  196.0 11.0 %collective-permute-done = bf16[1,512,256]{2,1,0:T(8,128)(2,1)} collective-permute-done((bf16[1,512,256]{2,1,0:T(8,128)(2,1)}, bf16[1,512,256]{2,1,0:T(8,128)(2,1)}, u32[]{:S(2)}, u32[]{:S(2)}) %collective-permute-start) | collective-permute-done | bytes 262176 | tf_op jit(solution)/shard_map/ppermute | solution.py:15
  207.1 2.3 %pad_maximum_fusion = bf16[6,512,256]{2,1,0:T(8,128)(2,1)} fusion(bf16[1,512,256]{2,1,0:T(8,128)(2,1)S(1)} %collective-permute-done.1, bf16[4,512,256]{2,1,0:T(8,128)(2,1)S(1)} %copy-done.1, bf16[1,512,256]{2,1,0:T(8,128)(2,1)} %collective-permute-done), kind=kLoop, calls=%fused_computation.11 | loop fusion | flops 1572864 | bytes 3145728 | tf_op jit(solution)/shard_map/concatenate | solution.py:13
  209.4 4.2 %gather_fusion = bf16[16,512,256]{2,1,0:T(8,128)(2,1)} fusion(bf16[6,512,256]{2,1,0:T(8,128)(2,1)} %pad_maximum_fusion, s32[1024]{0:T(1024)S(1)} %pad_clamp_fusion.2), kind=kCustom, calls=%fused_computation | custom fusion | bytes 8388672 | tf_op jit(solution)/shard_map/jit(_take)/gather | solution.py:38
  213.6 2.2 gather_fusion.2
  215.7 1.5 fusion.17
  217.3 4.5 %fusion.3 = bf16[4,512,256]{2,1,0:T(8,128)(2,1)} fusion(f32[4,512,256,1]{2,1,3,0:T(8,128)S(1)} %fusion.17, bf16[4,4,256,256]{3,2,1,0:T(8,128)(2,1)S(1)} %copy-done, bf16[4,4,512,256]{3,2,1,0:T(8,128)(2,1)} %bitcast.36, pred[4,4]{1,0:T(4,128)(4,1)S(1)} %compare_and_fusion.2), kind=kOutput, calls=%fused_computation.8 | convolution fusion | flops 1076887552 | bytes 9437200 | tf_op jit(solution)/shard_map/jerb,jebc->jrc/dot_general | solution.py:39
  (29 shorter events, 0.3 us)
Async XLA Ops:
  6.5 210.7 %copy-start = (bf16[4,4,256,256]{3,2,1,0:T(8,128)(2,1)S(1)}, bf16[4,4,256,256]{3,2,1,0:T(8,128)(2,1)}, u32[]{:S(2)}) copy-start(bf16[4,4,256,256]{3,2,1,0:T(8,128)(2,1)} %param.9) | copy-start | bytes 6291460
  6.5 51.4 %reduce-scatter.2.cloned.1.call-start = ((), (), s32[]{:S(2)}) async-start(), calls=%async_computation.1 | async-start | bytes 3932160 | tf_op jit(solution)/shard_map/reduce_scatter | solution.py:40
  9.9 2.9 %copy-start.4 = (s32[4,2]{0,1:T(2,128)S(1)}, s32[4,2]{0,1:T(2,128)}, u32[]{:S(2)}) copy-start(s32[4,2]{0,1:T(2,128)} %param.10) | copy-start | bytes 100
  19.6 139.9 %all-gather.9.cloned.1.call-start = ((), (), s32[]{:S(2)}) async-start(), calls=%async_computation.4 | async-start | bytes 7077888 | tf_op jit(solution)/shard_map/all_gather | solution.py:41
  58.0 123.4 %all-gather.5.cloned.1.call-start = ((), (), s32[]{:S(2)}) async-start(), calls=%async_computation.2 | async-start | bytes 1966080 | tf_op jit(solution)/shard_map/all_gather | solution.py:43
  159.4 4.0 %copy-start.2 = (s32[3,4]{1,0:T(4,128)S(1)}, s32[3,4]{1,0:T(4,128)}, u32[]{:S(2)}) copy-start(s32[3,4]{1,0:T(4,128)} %param.12) | copy-start | bytes 148
  163.4 50.1 %all-gather.7.cloned.1.call-start = ((), (), s32[]{:S(2)}) async-start(), calls=%async_computation.3 | async-start | bytes 1966080 | tf_op jit(solution)/shard_map/all_gather | solution.py:45
  184.8 3.0 %copy-start.1 = (bf16[4,512,256]{2,1,0:T(8,128)(2,1)S(1)}, bf16[4,512,256]{2,1,0:T(8,128)(2,1)}, u32[]{:S(2)}) copy-start(bf16[4,512,256]{2,1,0:T(8,128)(2,1)} %param.7) | copy-start | bytes 3145732
  184.8 9.2 %copy-start.3 = (s32[4,4]{1,0:T(4,128)S(1)}, s32[4,4]{1,0:T(4,128)}, u32[]{:S(2)}) copy-start(s32[4,4]{1,0:T(4,128)} %param.8) | copy-start | bytes 196
  188.6 7.4 %collective-permute-start.1 = (bf16[1,512,256]{2,1,0:T(8,128)(2,1)}, bf16[1,512,256]{2,1,0:T(8,128)(2,1)S(1)}, u32[]{:S(2)}, u32[]{:S(2)}) collective-permute-start(bf16[1,512,256]{2,1,0:T(8,128)(2,1)} %get-tuple-element.6), channel_id=1, source_target_pairs={{1,0},{2,1},{3,2},{4,3},{5,4},{6,5},{7,6},{8,7},{9,8},{10,9},{11,1... | collective-permute-start | bytes 786440 | tf_op jit(solution)/shard_map/ppermute | solution.py:17
  191.8 15.3 %collective-permute-start = (bf16[1,512,256]{2,1,0:T(8,128)(2,1)}, bf16[1,512,256]{2,1,0:T(8,128)(2,1)}, u32[]{:S(2)}, u32[]{:S(2)}) collective-permute-start(bf16[1,512,256]{2,1,0:T(8,128)(2,1)} %get-tuple-element.5), channel_id=1, source_target_pairs={{0,1},{1,2},{2,3},{3,4},{4,5},{5,6},{6,7},{7,8},{8,9},{9,10},{10,1... | collective-permute-start | bytes 786440 | tf_op jit(solution)/shard_map/ppermute | solution.py:15
Sparse Core Ops, SparseCore 0:
  19.7 38.1 reduce-scatter.1
  60.4 99.0 all-gather.8
  163.5 17.8 all-gather.4
  187.8 23.5 all-gather.6
